TPU v7x, 256 devices: a whole 4x4x8 slice. The times are simulated.
256 devices in a mesh: scen: 8 (over y, z_hi), grid: 32 (over x, z_lo, core).
Axes of the slice: x: 4, y: 4, z: 8 (z_hi: 2, z_lo: 4; z = z_hi * 4 + z_lo), core: 2. Of those that a mesh axis runs over, the one named last changes fastest.
Arguments:
- adjoint_in: float32 [16, 2, 50, 512, 128], P('scen', None, None, 'grid'), may hold values from -6 to 6
- surface_carbon: float32 [16, 512, 128], P('scen', 'grid'), may hold values from 1.9 to 2.1
- surface_alkalinity: float32 [16, 512, 128], P('scen', 'grid'), may hold values from 2.2 to 2.4
- east_velocity: float32 [50, 512, 128], P(None, 'grid'), may hold values from -0.1 to 0.1
- north_velocity: float32 [50, 512, 128], P(None, 'grid'), may hold values from -0.1 to 0.1
- east_diffusion: float32 [50], replicated, may hold values from 0.08 to 0.25
- north_diffusion: float32 [50], replicated, may hold values from 0.02 to 0.1
- vertical_mix: float32 [50, 512, 128], P(None, 'grid'), may hold values from 0.05 to 5
- thickness: float32 [50], replicated, may hold values from 0.5 to 4
- export_flux: float32 [50, 512, 128], P(None, 'grid'), may hold values from 0.1 to 1
- piston: float32 [512, 128], P('grid'), may hold values from 0.0005 to 0.005
- wet_mask: int32 [512, 128], P('grid'), may hold values 0 or 1
- bottom_level: int32 [512, 128], P('grid'), may hold values from 41 to 50
Outputs:
- adjoint_out: float32 [16, 2, 50, 512, 128], P('scen', None, None, 'grid')
- rate_gradient: float32 [50, 512, 128], P(None, 'grid')
All inputs are finite; a program needn't handle non-finite values. No bound on the sum of `wet_mask` on one device may be relied on, other than what follows from the above.
Results may differ from a plain program's by a relative error of at most 0.00002.
Values sent between devices are 32-bit elements; how exact they have to be, the bound alone decides.
No kernel may reach another device: no remote copies, remote signals or barrier semaphores. Data moves between devices by JAX's collectives and lax.ppermute only.
A program may use at most 64 MiB of HBM per device.

v0:
```python
import jax
import jax.numpy as jnp
from jax import lax
from jax.sharding import PartitionSpec as P

SUBSTEPS = 6
alk_ratio = 0.137


def extended(array, sides, width):
    for axis, dim in sides:
        size, length = (lax.axis_size(axis), array.shape[dim])
        up = [(i, (i + 1) % size) for i in range(size)]
        down = [(j, i) for i, j in up]
        last = lax.slice_in_dim(array, length - width, length, axis=dim)
        initial = lax.slice_in_dim(array, 0, width, axis=dim)
        before = lax.ppermute(last, axis, up)
        after = lax.ppermute(initial, axis, down)
        array = jnp.concatenate([before, array, after], axis=dim)
    return array


def wet_cells(wet_mask, bottom_level, levels):
    depth_index = lax.broadcasted_iota(jnp.int32, (levels,) + wet_mask.shape, 0)
    return ((wet_mask[None] > 0) & (depth_index < bottom_level[None])).astype(jnp.float32)


def face_pairs(velocity, mask_here, mask_next, diffusion):
    opened = mask_here * mask_next
    moving = velocity * opened
    mixing = diffusion[:, None, None] * opened
    return (mixing + jnp.maximum(moving, 0.0), jnp.minimum(moving, 0.0) - mixing)


def north_transpose(adjoint, upwind, downwind):
    zero_column = jnp.zeros(adjoint.shape[:-1] + (1,), jnp.float32)
    zero_face = jnp.zeros(upwind.shape[:-1] + (1,), jnp.float32)
    ahead = jnp.concatenate([adjoint[..., 1:], zero_column], -1)
    behind = jnp.concatenate([zero_column, adjoint[..., :-1]], -1)
    upwind_full = jnp.concatenate([upwind, zero_face], -1)
    downwind_full = jnp.concatenate([zero_face, downwind], -1)
    return upwind_full * (adjoint - ahead) + downwind_full * (behind - adjoint)


def column_coefficients(vertical_mix, thickness, wet_cube):
    zero_layer = jnp.zeros((1,) + wet_cube.shape[1:], jnp.float32)
    opened = jnp.concatenate([wet_cube[:-1] * wet_cube[1:], zero_layer], 0)
    mixing = vertical_mix * opened
    mixing_above = jnp.concatenate([zero_layer, mixing[:-1]], 0)
    height = thickness[:, None, None]
    height_above = jnp.concatenate([thickness[:1], thickness[:-1]])[:, None, None]
    height_below = jnp.concatenate([thickness[1:], thickness[-1:]])[:, None, None]
    diagonal = 1.0 + (mixing + mixing_above) / height
    below_band = -mixing_above / height_above
    above_band = -mixing / height_below
    return (below_band, diagonal, above_band)


def transposed_solve(right_side, below_band, diagonal, above_band):
    levels = diagonal.shape[0]
    pivots = diagonal[0]
    factors = [above_band[0] / pivots]
    reduced = [right_side[..., 0, :, :] / pivots]
    for level in range(1, levels):
        pivots = diagonal[level] - below_band[level] * factors[-1]
        factors.append(above_band[level] / pivots)
        reduced.append((right_side[..., level, :, :] - below_band[level] * reduced[-1]) / pivots)
    solved = [reduced[-1]]
    for level in range(levels - 2, -1, -1):
        solved.append(reduced[level] - factors[level] * solved[-1])
    return jnp.stack(solved[::-1], axis=-3)


def carbonate_slopes(carbon, alkalinity):
    excess = 2.0 * carbon - alkalinity
    spread = alkalinity - carbon
    square = spread * spread
    return (
        (4.0 * excess * spread + excess * excess) / square,
        (-2.0 * excess * spread - excess * excess) / square,
    )


def on_device(
    adjoint_in,
    surface_carbon,
    surface_alkalinity,
    east_velocity,
    north_velocity,
    east_diffusion,
    north_diffusion,
    vertical_mix,
    thickness,
    export_flux,
    piston,
    wet_mask,
    bottom_level,
):
    levels = vertical_mix.shape[0]
    wet_cube = wet_cells(wet_mask, bottom_level, levels)
    below_band, diagonal, above_band = column_coefficients(vertical_mix, thickness, wet_cube)
    adjoint = transposed_solve(adjoint_in, below_band, diagonal, above_band)
    stacked = jnp.stack([east_velocity, wet_cube])
    widened = extended(stacked, (("grid", 2),), 1)
    east_a, east_b = face_pairs(
        widened[0][:, :-1], widened[1][:, :-1], widened[1][:, 1:], east_diffusion
    )
    north_a, north_b = face_pairs(
        north_velocity[:, :, :-1], wet_cube[:, :, :-1], wet_cube[:, :, 1:], north_diffusion
    )
    for repeat in range(SUBSTEPS):
        wide_adjoint = extended(adjoint, (("grid", 3),), 1)
        centre = wide_adjoint[..., 1:-1, :]
        adjoint = (
            centre
            - east_a[:, 1:] * (centre - wide_adjoint[..., 2:, :])
            - east_b[:, :-1] * (wide_adjoint[..., :-2, :] - centre)
            - north_transpose(centre, north_a, north_b)
        )
    rate_term = jnp.sum(adjoint[:, 0] - alk_ratio * adjoint[:, 1], axis=0)
    summed = lax.psum(rate_term, "scen")
    rate_gradient = export_flux * wet_cube * summed
    slope_carbon, slope_alkalinity = carbonate_slopes(surface_carbon, surface_alkalinity)
    exchange_scale = wet_cube[0] * piston * adjoint[:, 0, 0]
    adjoint = (
        adjoint.at[:, 0, 0]
        .add(-exchange_scale * slope_carbon)
        .at[:, 1, 0]
        .add(-exchange_scale * slope_alkalinity)
    )
    return (adjoint, rate_gradient)


def solution(mesh):
    in_specs = (
        P("scen", None, None, "grid", None),
        P("scen", "grid", None),
        P("scen", "grid", None),
        P(None, "grid", None),
        P(None, "grid", None),
        P(),
        P(),
        P(None, "grid", None),
        P(),
        P(None, "grid", None),
        P("grid", None),
        P("grid", None),
        P("grid", None),
    )
    out_specs = (P("scen", None, None, "grid", None), P(None, "grid", None))
    return jax.shard_map(
        on_device, mesh=mesh, in_specs=in_specs, out_specs=out_specs, check_vma=False
    )
```

profile of v0, /device:TPU:2, one launch (start us, length us, event | category | flops | bytes accessed | tf_op | source)
XLA Modules:
  0.0 205.5 jit_solution(14609413593430815188)
XLA Ops:
  7.2 1.3 fusion.358
  8.5 0.8 fusion.359
  9.3 0.7 broadcast_compare_fusion
  10.0 0.8 fusion.45
  10.8 1.4 pad_maximum_fusion.15
  12.2 0.1 negate_divide_fusion.1
  12.4 0.2 negate_divide_fusion
  12.7 1.1 copy-done
  14.0 0.5 fusion.146
  14.5 0.6 constant_dynamic-update-slice_fusion.49
  15.7 0.8 constant_dynamic-update-slice_fusion.6
  16.5 0.1 fusion.354
  16.7 4.1 %collective-permute-start.2 = (f32[2,2,50,1,128]{4,3,0,2,1:T(1,128)S(1)}, f32[2,2,50,1,128]{4,3,0,2,1:T(1,128)S(1)}, u32[]{:S(2)}, u32[]{:S(2)}) collective-permute-start(f32[2,2,50,1,128]{4,3,0,2,1:T(1,128)S(1)} %get-tuple-element.196), channel_id=1, source_target_pairs={{1,0},{2,1},{3,2},{4,3},{5,4},{6,5},{7,6},{8,7},{9,8},{10,9},{11,1... | collective-permute-start | bytes 307208 | tf_op jit(solution)/shard_map/ppermute | solution.py:18
  20.9 0.1 collective-permute-start
  21.0 4.5 %collective-permute-start.1 = (f32[2,50,1,128]{3,2,1,0:T(1,128)S(1)}, f32[2,50,1,128]{3,2,1,0:T(1,128)S(1)}, u32[]{:S(2)}, u32[]{:S(2)}) collective-permute-start(f32[2,50,1,128]{3,2,1,0:T(1,128)S(1)} %get-tuple-element.255), channel_id=1, source_target_pairs={{1,0},{2,1},{3,2},{4,3},{5,4},{6,5},{7,6},{8,7},{9,8},{10,9},{11,1... | collective-permute-start | bytes 153608 | tf_op jit(solution)/shard_map/ppermute | solution.py:18
  25.6 0.6 fusion.353
  26.2 0.2 maximum_add_fusion
  26.4 0.5 copy-done.8
  26.9 0.2 concatenate.123
  27.1 1.6 collective-permute-done
  28.7 0.2 pad_maximum_fusion.12
  28.9 0.1 slice_bitcast_fusion
  29.0 0.6 copy-done.10
  29.5 0.1 slice_multiply_fusion.1
  29.7 0.1 slice_add_fusion
  29.8 1.2 fusion.38
  31.1 0.1 fusion.352
  31.2 3.2 %collective-permute-start.4 = (f32[2,2,50,1,128]{4,3,0,2,1:T(1,128)S(1)}, f32[2,2,50,1,128]{4,3,0,2,1:T(1,128)S(1)}, u32[]{:S(2)}, u32[]{:S(2)}) collective-permute-start(f32[2,2,50,1,128]{4,3,0,2,1:T(1,128)S(1)} %get-tuple-element.192), channel_id=1, source_target_pairs={{1,0},{2,1},{3,2},{4,3},{5,4},{6,5},{7,6},{8,7},{9,8},{10,9},{11,1... | collective-permute-start | bytes 307208 | tf_op jit(solution)/shard_map/ppermute | solution.py:18
  34.4 0.6 fusion.351
  35.0 1.6 collective-permute-done.4
  36.7 5.2 %collective-permute-done.5 = f32[2,2,50,1,128]{4,3,0,2,1:T(1,128)S(1)} collective-permute-done((f32[2,2,50,1,128]{4,3,0,2,1:T(1,128)S(1)}, f32[2,2,50,1,128]{4,3,0,2,1:T(1,128)S(1)}, u32[]{:S(2)}, u32[]{:S(2)}) %collective-permute-start.5) | collective-permute-done | bytes 102432 | tf_op jit(solution)/shard_map/ppermute | solution.py:17
  41.8 1.2 fusion.31
  43.1 0.1 fusion.350
  43.2 0.1 collective-permute-start.6
  43.3 0.5 collective-permute-start.7
  43.8 0.6 fusion.349
  44.4 2.0 collective-permute-done.6
  46.4 3.9 %collective-permute-done.7 = f32[2,2,50,1,128]{4,3,0,2,1:T(1,128)S(1)} collective-permute-done((f32[2,2,50,1,128]{4,3,0,2,1:T(1,128)S(1)}, f32[2,2,50,1,128]{4,3,0,2,1:T(1,128)S(1)}, u32[]{:S(2)}, u32[]{:S(2)}) %collective-permute-start.7) | collective-permute-done | bytes 102432 | tf_op jit(solution)/shard_map/ppermute | solution.py:17
  50.3 1.2 fusion.24
  51.5 0.1 fusion.348
  51.6 0.9 collective-permute-start.8
  52.5 0.6 fusion.347
  53.2 1.7 collective-permute-done.8
  54.8 4.5 %collective-permute-done.9 = f32[2,2,50,1,128]{4,3,0,2,1:T(1,128)S(1)} collective-permute-done((f32[2,2,50,1,128]{4,3,0,2,1:T(1,128)S(1)}, f32[2,2,50,1,128]{4,3,0,2,1:T(1,128)S(1)}, u32[]{:S(2)}, u32[]{:S(2)}) %collective-permute-start.9) | collective-permute-done | bytes 102432 | tf_op jit(solution)/shard_map/ppermute | solution.py:17
  59.3 1.2 fusion.17
  60.5 0.1 fusion.346
  60.7 0.2 collective-permute-start.10
  60.9 0.4 collective-permute-start.11
  61.3 0.6 fusion.345
  61.9 2.0 collective-permute-done.10
  63.9 4.0 %collective-permute-done.11 = f32[2,2,50,1,128]{4,3,0,2,1:T(1,128)S(1)} collective-permute-done((f32[2,2,50,1,128]{4,3,0,2,1:T(1,128)S(1)}, f32[2,2,50,1,128]{4,3,0,2,1:T(1,128)S(1)}, u32[]{:S(2)}, u32[]{:S(2)}) %collective-permute-start.11) | collective-permute-done | bytes 102432 | tf_op jit(solution)/shard_map/ppermute | solution.py:17
  67.9 1.2 fusion.10
  69.1 0.1 fusion.344
  69.2 0.8 collective-permute-start.12
  70.0 0.6 fusion.343
  70.6 1.8 collective-permute-done.12
  72.4 4.4 %collective-permute-done.13 = f32[2,2,50,1,128]{4,3,0,2,1:T(1,128)S(1)} collective-permute-done((f32[2,2,50,1,128]{4,3,0,2,1:T(1,128)S(1)}, f32[2,2,50,1,128]{4,3,0,2,1:T(1,128)S(1)}, u32[]{:S(2)}, u32[]{:S(2)}) %collective-permute-start.13) | collective-permute-done | bytes 102432 | tf_op jit(solution)/shard_map/ppermute | solution.py:17
  76.8 1.2 fusion.3
  78.1 0.1 copy.491
  78.2 1.0 fusion.43
  79.3 1.3 copy.115
  80.6 0.6 fusion.142
  81.2 115.5 %all-reduce.18.cloned.1.call-done = f32[50,16,128]{2,1,0:T(8,128)} async-done(((f32[50,16,128]{2,1,0:T(8,128)}), f32[50,16,128]{2,1,0:T(8,128)}) %all-reduce.18.cloned.1.call-update) | async-done | bytes 409616 | tf_op jit(solution)/shard_map/psum | solution.py:121
  196.7 2.0 select_multiply_fusion
  (92 shorter events, 1.0 us)
Async XLA Ops:
  7.2 5.0 %copy-start.2 = (f32[50,16,128]{2,1,0:T(8,128)S(1)}, f32[50,16,128]{2,1,0:T(8,128)}, u32[]{:S(2)}) copy-start(f32[50,16,128]{2,1,0:T(8,128)} %param.24) | copy-start | bytes 1228804
  7.2 189.5 %all-reduce.18.cloned.1.call-start = ((), (), s32[]{:S(2)}) async-start(), calls=%async_computation | async-start | bytes 819200 | tf_op jit(solution)/shard_map/psum | solution.py:121
  10.8 1.6 copy-start.7
  12.3 1.4 copy-start
  15.6 5.1 %copy-start.4 = (s32[16,128]{1,0:T(8,128)S(1)}, s32[16,128]{1,0:T(8,128)}, u32[]{:S(2)}) copy-start(s32[16,128]{1,0:T(8,128)} %param.29) | copy-start | bytes 24580
  15.7 5.2 %copy-start.1 = (f32[50,16,128]{2,1,0:T(8,128)S(1)}, f32[50,16,128]{2,1,0:T(8,128)}, u32[]{:S(2)}) copy-start(f32[50,16,128]{2,1,0:T(8,128)} %param.20) | copy-start | bytes 1228804
  16.7 13.2 %collective-permute-start.2 = (f32[2,2,50,1,128]{4,3,0,2,1:T(1,128)S(1)}, f32[2,2,50,1,128]{4,3,0,2,1:T(1,128)S(1)}, u32[]{:S(2)}, u32[]{:S(2)}) collective-permute-start(f32[2,2,50,1,128]{4,3,0,2,1:T(1,128)S(1)} %get-tuple-element.196), channel_id=1, source_target_pairs={{1,0},{2,1},{3,2},{4,3},{5,4},{6,5},{7,6},{8,7},{9,8},{10,9},{11,1... | collective-permute-start | bytes 307208 | tf_op jit(solution)/shard_map/ppermute | solution.py:18
  20.8 9.0 %collective-permute-start.3 = (f32[2,2,50,1,128]{4,3,0,2,1:T(1,128)S(1)}, f32[2,2,50,1,128]{4,3,0,2,1:T(1,128)S(1)}, u32[]{:S(2)}, u32[]{:S(2)}) collective-permute-start(f32[2,2,50,1,128]{4,3,0,2,1:T(1,128)S(1)} %get-tuple-element.197), channel_id=1, source_target_pairs={{0,1},{1,2},{2,3},{3,4},{4,5},{5,6},{6,7},{7,8},{8,9},{9,10},{10,1... | collective-permute-start | bytes 307208 | tf_op jit(solution)/shard_map/ppermute | solution.py:17
  20.9 7.7 %collective-permute-start = (f32[2,50,1,128]{3,2,1,0:T(1,128)S(1)}, f32[2,50,1,128]{3,2,1,0:T(1,128)S(1)}, u32[]{:S(2)}, u32[]{:S(2)}) collective-permute-start(f32[2,50,1,128]{3,2,1,0:T(1,128)S(1)} %get-tuple-element.254), channel_id=1, source_target_pairs={{0,1},{1,2},{2,3},{3,4},{4,5},{5,6},{6,7},{7,8},{8,9},{9,10},{10,1... | collective-permute-start | bytes 153608 | tf_op jit(solution)/shard_map/ppermute | solution.py:17
  21.0 5.2 %copy-start.3 = (f32[50,16,128]{2,1,0:T(8,128)S(1)}, f32[50,16,128]{2,1,0:T(8,128)}, u32[]{:S(2)}) copy-start(f32[50,16,128]{2,1,0:T(8,128)} %param.21) | copy-start | bytes 1228804
  21.0 5.1 %copy-start.9 = (f32[50]{0:T(128)S(1)}, f32[50]{0:T(128)}, u32[]{:S(2)}) copy-start(f32[50]{0:T(128)} %param.23) | copy-start | bytes 604
  21.0 7.6 %collective-permute-start.1 = (f32[2,50,1,128]{3,2,1,0:T(1,128)S(1)}, f32[2,50,1,128]{3,2,1,0:T(1,128)S(1)}, u32[]{:S(2)}, u32[]{:S(2)}) collective-permute-start(f32[2,50,1,128]{3,2,1,0:T(1,128)S(1)} %get-tuple-element.255), channel_id=1, source_target_pairs={{1,0},{2,1},{3,2},{4,3},{5,4},{6,5},{7,6},{8,7},{9,8},{10,9},{11,1... | collective-permute-start | bytes 153608 | tf_op jit(solution)/shard_map/ppermute | solution.py:18
  26.2 0.7 copy-start.8
  28.9 0.7 copy-start.10
  31.2 5.5 %collective-permute-start.4 = (f32[2,2,50,1,128]{4,3,0,2,1:T(1,128)S(1)}, f32[2,2,50,1,128]{4,3,0,2,1:T(1,128)S(1)}, u32[]{:S(2)}, u32[]{:S(2)}) collective-permute-start(f32[2,2,50,1,128]{4,3,0,2,1:T(1,128)S(1)} %get-tuple-element.192), channel_id=1, source_target_pairs={{1,0},{2,1},{3,2},{4,3},{5,4},{6,5},{7,6},{8,7},{9,8},{10,9},{11,1... | collective-permute-start | bytes 307208 | tf_op jit(solution)/shard_map/ppermute | solution.py:18
  34.4 7.4 %collective-permute-start.5 = (f32[2,2,50,1,128]{4,3,0,2,1:T(1,128)S(1)}, f32[2,2,50,1,128]{4,3,0,2,1:T(1,128)S(1)}, u32[]{:S(2)}, u32[]{:S(2)}) collective-permute-start(f32[2,2,50,1,128]{4,3,0,2,1:T(1,128)S(1)} %get-tuple-element.193), channel_id=1, source_target_pairs={{0,1},{1,2},{2,3},{3,4},{4,5},{5,6},{6,7},{7,8},{8,9},{9,10},{10,1... | collective-permute-start | bytes 307208 | tf_op jit(solution)/shard_map/ppermute | solution.py:17
  43.2 3.2 %collective-permute-start.6 = (f32[2,2,50,1,128]{4,3,0,2,1:T(1,128)S(1)}, f32[2,2,50,1,128]{4,3,0,2,1:T(1,128)S(1)}, u32[]{:S(2)}, u32[]{:S(2)}) collective-permute-start(f32[2,2,50,1,128]{4,3,0,2,1:T(1,128)S(1)} %get-tuple-element.188), channel_id=1, source_target_pairs={{1,0},{2,1},{3,2},{4,3},{5,4},{6,5},{7,6},{8,7},{9,8},{10,9},{11,1... | collective-permute-start | bytes 307208 | tf_op jit(solution)/shard_map/ppermute | solution.py:18
  43.3 7.0 %collective-permute-start.7 = (f32[2,2,50,1,128]{4,3,0,2,1:T(1,128)S(1)}, f32[2,2,50,1,128]{4,3,0,2,1:T(1,128)S(1)}, u32[]{:S(2)}, u32[]{:S(2)}) collective-permute-start(f32[2,2,50,1,128]{4,3,0,2,1:T(1,128)S(1)} %get-tuple-element.189), channel_id=1, source_target_pairs={{0,1},{1,2},{2,3},{3,4},{4,5},{5,6},{6,7},{7,8},{8,9},{9,10},{10,1... | collective-permute-start | bytes 307208 | tf_op jit(solution)/shard_map/ppermute | solution.py:17
  51.6 3.2 %collective-permute-start.8 = (f32[2,2,50,1,128]{4,3,0,2,1:T(1,128)S(1)}, f32[2,2,50,1,128]{4,3,0,2,1:T(1,128)S(1)}, u32[]{:S(2)}, u32[]{:S(2)}) collective-permute-start(f32[2,2,50,1,128]{4,3,0,2,1:T(1,128)S(1)} %get-tuple-element.184), channel_id=1, source_target_pairs={{1,0},{2,1},{3,2},{4,3},{5,4},{6,5},{7,6},{8,7},{9,8},{10,9},{11,1... | collective-permute-start | bytes 307208 | tf_op jit(solution)/shard_map/ppermute | solution.py:18
  52.5 6.8 %collective-permute-start.9 = (f32[2,2,50,1,128]{4,3,0,2,1:T(1,128)S(1)}, f32[2,2,50,1,128]{4,3,0,2,1:T(1,128)S(1)}, u32[]{:S(2)}, u32[]{:S(2)}) collective-permute-start(f32[2,2,50,1,128]{4,3,0,2,1:T(1,128)S(1)} %get-tuple-element.185), channel_id=1, source_target_pairs={{0,1},{1,2},{2,3},{3,4},{4,5},{5,6},{6,7},{7,8},{8,9},{9,10},{10,1... | collective-permute-start | bytes 307208 | tf_op jit(solution)/shard_map/ppermute | solution.py:17
  60.7 3.2 %collective-permute-start.10 = (f32[2,2,50,1,128]{4,3,0,2,1:T(1,128)S(1)}, f32[2,2,50,1,128]{4,3,0,2,1:T(1,128)S(1)}, u32[]{:S(2)}, u32[]{:S(2)}) collective-permute-start(f32[2,2,50,1,128]{4,3,0,2,1:T(1,128)S(1)} %get-tuple-element.180), channel_id=1, source_target_pairs={{1,0},{2,1},{3,2},{4,3},{5,4},{6,5},{7,6},{8,7},{9,8},{10,9},{11,1... | collective-permute-start | bytes 307208 | tf_op jit(solution)/shard_map/ppermute | solution.py:18
  60.9 7.0 %collective-permute-start.11 = (f32[2,2,50,1,128]{4,3,0,2,1:T(1,128)S(1)}, f32[2,2,50,1,128]{4,3,0,2,1:T(1,128)S(1)}, u32[]{:S(2)}, u32[]{:S(2)}) collective-permute-start(f32[2,2,50,1,128]{4,3,0,2,1:T(1,128)S(1)} %get-tuple-element.181), channel_id=1, source_target_pairs={{0,1},{1,2},{2,3},{3,4},{4,5},{5,6},{6,7},{7,8},{8,9},{9,10},{10,1... | collective-permute-start | bytes 307208 | tf_op jit(solution)/shard_map/ppermute | solution.py:17
  69.2 3.2 %collective-permute-start.12 = (f32[2,2,50,1,128]{4,3,0,2,1:T(1,128)S(1)}, f32[2,2,50,1,128]{4,3,0,2,1:T(1,128)S(1)}, u32[]{:S(2)}, u32[]{:S(2)}) collective-permute-start(f32[2,2,50,1,128]{4,3,0,2,1:T(1,128)S(1)} %get-tuple-element.176), channel_id=1, source_target_pairs={{1,0},{2,1},{3,2},{4,3},{5,4},{6,5},{7,6},{8,7},{9,8},{10,9},{11,1... | collective-permute-start | bytes 307208 | tf_op jit(solution)/shard_map/ppermute | solution.py:18
  70.0 6.8 %collective-permute-start.13 = (f32[2,2,50,1,128]{4,3,0,2,1:T(1,128)S(1)}, f32[2,2,50,1,128]{4,3,0,2,1:T(1,128)S(1)}, u32[]{:S(2)}, u32[]{:S(2)}) collective-permute-start(f32[2,2,50,1,128]{4,3,0,2,1:T(1,128)S(1)} %get-tuple-element.177), channel_id=1, source_target_pairs={{0,1},{1,2},{2,3},{3,4},{4,5},{5,6},{6,7},{7,8},{8,9},{9,10},{10,1... | collective-permute-start | bytes 307208 | tf_op jit(solution)/shard_map/ppermute | solution.py:17
  78.2 1.0 copy-start.5
  78.2 1.0 copy-start.6
Sparse Core Ops, SparseCore 0:
  79.3 117.3 all-reduce.17
where the time goes:
time: 206 us
  waiting for transfers between devices  148 us (72%)
  other arithmetic  16.9 us (8%)
  starting transfers between devices  14.8 us (7%)
  between operations  14.8 us (7%)
  local copies, waits for them, and re-layouts  10.9 us (5%)
    psum x1, waiting for transfers between devices, on_device(): summed = lax.psum(rate_term, 'scen')  116 us
    ppermute x7, waiting for transfers between devices, extended(): before = lax.ppermute(last, axis, up)  23.5 us
    ppermute x7, starting transfers between devices, extended(): after = lax.ppermute(initial, axis, down)  13.8 us
    ppermute x7, waiting for transfers between devices, extended(): after = lax.ppermute(initial, axis, down)  9.04 us
    sub x6, other arithmetic, on_device(): centre - east_a[:, 1:] * (centre - wide_adjoint[..., 2:, :])  7.31 us
  transfers between devices with their start and end apart: 15, of which 12 were waited for; matrix products, arithmetic and copies ran while one was open for 3% of the time, Pallas kernels for 0%

commit v1 on v0

--- a/solution.py
+++ b/solution.py
@@ -118,7 +118,7 @@
             - north_transpose(centre, north_a, north_b)
         )
     rate_term = jnp.sum(adjoint[:, 0] - alk_ratio * adjoint[:, 1], axis=0)
-    summed = lax.psum(rate_term, "scen")
+    summed = jnp.sum(lax.all_gather(rate_term, "scen"), axis=0)
     rate_gradient = export_flux * wet_cube * summed
     slope_carbon, slope_alkalinity = carbonate_slopes(surface_carbon, surface_alkalinity)
     exchange_scale = wet_cube[0] * piston * adjoint[:, 0, 0]

time: 206 us -> 191 us (0.927)
  waiting for transfers between devices: 148 us -> 134 us
    psum x1 -> x0, waiting for transfers between devices: 116 us -> none  [on_device(): summed = lax.psum(rate_term, 'scen')]
    all_gather x0 -> x1, waiting for transfers between devices: none -> 100 us  [on_device(): summed = jnp.sum(lax.all_gather(rate_term, 'scen'), axis=0)]
    reduce_sum x0 -> x1, other arithmetic: none -> 2.23 us  [on_device(): summed = jnp.sum(lax.all_gather(rate_term, 'scen'), axis=0)]
where the time goes in v1:
time: 191 us; the launch traced here: 190 us
  waiting for transfers between devices  134 us (70%)
  other arithmetic  17.5 us (9%)
  starting transfers between devices  14.8 us (8%)
  between operations  14.8 us (8%)
  local copies, waits for them, and re-layouts  9.77 us (5%)
    all_gather x1, waiting for transfers between devices, on_device(): summed = jnp.sum(lax.all_gather(rate_term, 'scen'), axis=0)  100 us
    ppermute x7, waiting for transfers between devices, extended(): before = lax.ppermute(last, axis, up)  24 us
    ppermute x7, starting transfers between devices, extended(): after = lax.ppermute(initial, axis, down)  13.8 us
    ppermute x7, waiting for transfers between devices, extended(): after = lax.ppermute(initial, axis, down)  9.04 us
    sub x6, other arithmetic, on_device(): centre - east_a[:, 1:] * (centre - wide_adjoint[..., 2:, :])  7.35 us
  transfers between devices with their start and end apart: 15, of which 12 were waited for; matrix products, arithmetic and copies ran while one was open for 3% of the time, Pallas kernels for 0%

profile of v1, /device:TPU:2, one launch (start us, length us, event | category | flops | bytes accessed | tf_op | source)
XLA Modules:
  0.0 190.4 jit_solution(2570459996005765170)
XLA Ops:
  7.2 1.3 fusion.358
  8.5 0.8 fusion.359
  9.3 0.7 broadcast_compare_fusion
  10.0 0.8 fusion.45
  10.8 1.4 pad_maximum_fusion.15
  12.2 0.1 negate_divide_fusion.1
  12.4 0.2 negate_divide_fusion
  12.7 1.1 copy-done
  14.0 0.5 fusion.146
  14.5 0.5 constant_dynamic-update-slice_fusion.49
  15.6 0.8 constant_dynamic-update-slice_fusion.6
  16.5 0.1 fusion.354
  16.6 4.1 %collective-permute-start.2 = (f32[2,2,50,1,128]{4,3,0,2,1:T(1,128)S(1)}, f32[2,2,50,1,128]{4,3,0,2,1:T(1,128)S(1)}, u32[]{:S(2)}, u32[]{:S(2)}) collective-permute-start(f32[2,2,50,1,128]{4,3,0,2,1:T(1,128)S(1)} %get-tuple-element.196), channel_id=1, source_target_pairs={{1,0},{2,1},{3,2},{4,3},{5,4},{6,5},{7,6},{8,7},{9,8},{10,9},{11,1... | collective-permute-start | bytes 307208 | tf_op jit(solution)/shard_map/ppermute | solution.py:18
  20.9 0.1 collective-permute-start
  21.0 4.5 %collective-permute-start.1 = (f32[2,50,1,128]{3,2,1,0:T(1,128)S(1)}, f32[2,50,1,128]{3,2,1,0:T(1,128)S(1)}, u32[]{:S(2)}, u32[]{:S(2)}) collective-permute-start(f32[2,50,1,128]{3,2,1,0:T(1,128)S(1)} %get-tuple-element.255), channel_id=1, source_target_pairs={{1,0},{2,1},{3,2},{4,3},{5,4},{6,5},{7,6},{8,7},{9,8},{10,9},{11,1... | collective-permute-start | bytes 153608 | tf_op jit(solution)/shard_map/ppermute | solution.py:18
  25.5 0.6 fusion.353
  26.2 0.2 maximum_add_fusion
  26.5 0.2 concatenate.123
  26.6 2.0 %collective-permute-done = f32[2,50,1,128]{3,2,1,0:T(1,128)S(1)} collective-permute-done((f32[2,50,1,128]{3,2,1,0:T(1,128)S(1)}, f32[2,50,1,128]{3,2,1,0:T(1,128)S(1)}, u32[]{:S(2)}, u32[]{:S(2)}) %collective-permute-start) | collective-permute-done | bytes 51232 | tf_op jit(solution)/shard_map/ppermute | solution.py:17
  28.6 0.2 pad_maximum_fusion.12
  28.9 0.1 slice_bitcast_fusion
  28.9 0.6 copy-done.12
  29.5 0.1 slice_multiply_fusion.1
  29.6 0.1 slice_add_fusion
  29.8 1.3 fusion.38
  31.1 0.1 fusion.352
  31.2 3.2 %collective-permute-start.4 = (f32[2,2,50,1,128]{4,3,0,2,1:T(1,128)S(1)}, f32[2,2,50,1,128]{4,3,0,2,1:T(1,128)S(1)}, u32[]{:S(2)}, u32[]{:S(2)}) collective-permute-start(f32[2,2,50,1,128]{4,3,0,2,1:T(1,128)S(1)} %get-tuple-element.192), channel_id=1, source_target_pairs={{1,0},{2,1},{3,2},{4,3},{5,4},{6,5},{7,6},{8,7},{9,8},{10,9},{11,1... | collective-permute-start | bytes 307208 | tf_op jit(solution)/shard_map/ppermute | solution.py:18
  34.4 0.6 fusion.351
  35.0 1.6 collective-permute-done.4
  36.7 5.2 %collective-permute-done.5 = f32[2,2,50,1,128]{4,3,0,2,1:T(1,128)S(1)} collective-permute-done((f32[2,2,50,1,128]{4,3,0,2,1:T(1,128)S(1)}, f32[2,2,50,1,128]{4,3,0,2,1:T(1,128)S(1)}, u32[]{:S(2)}, u32[]{:S(2)}) %collective-permute-start.5) | collective-permute-done | bytes 102432 | tf_op jit(solution)/shard_map/ppermute | solution.py:17
  41.8 1.2 fusion.31
  43.1 0.1 fusion.350
  43.2 0.1 collective-permute-start.6
  43.3 0.5 collective-permute-start.7
  43.8 0.6 fusion.349
  44.4 2.0 %collective-permute-done.6 = f32[2,2,50,1,128]{4,3,0,2,1:T(1,128)S(1)} collective-permute-done((f32[2,2,50,1,128]{4,3,0,2,1:T(1,128)S(1)}, f32[2,2,50,1,128]{4,3,0,2,1:T(1,128)S(1)}, u32[]{:S(2)}, u32[]{:S(2)}) %collective-permute-start.6) | collective-permute-done | bytes 102432 | tf_op jit(solution)/shard_map/ppermute | solution.py:18
  46.4 3.9 %collective-permute-done.7 = f32[2,2,50,1,128]{4,3,0,2,1:T(1,128)S(1)} collective-permute-done((f32[2,2,50,1,128]{4,3,0,2,1:T(1,128)S(1)}, f32[2,2,50,1,128]{4,3,0,2,1:T(1,128)S(1)}, u32[]{:S(2)}, u32[]{:S(2)}) %collective-permute-start.7) | collective-permute-done | bytes 102432 | tf_op jit(solution)/shard_map/ppermute | solution.py:17
  50.3 1.2 fusion.24
  51.5 0.1 fusion.348
  51.6 0.9 collective-permute-start.8
  52.5 0.6 fusion.347
  53.2 1.7 collective-permute-done.8
  54.8 4.5 %collective-permute-done.9 = f32[2,2,50,1,128]{4,3,0,2,1:T(1,128)S(1)} collective-permute-done((f32[2,2,50,1,128]{4,3,0,2,1:T(1,128)S(1)}, f32[2,2,50,1,128]{4,3,0,2,1:T(1,128)S(1)}, u32[]{:S(2)}, u32[]{:S(2)}) %collective-permute-start.9) | collective-permute-done | bytes 102432 | tf_op jit(solution)/shard_map/ppermute | solution.py:17
  59.3 1.2 fusion.17
  60.5 0.1 fusion.346
  60.7 0.2 collective-permute-start.10
  60.9 0.4 collective-permute-start.11
  61.3 0.6 fusion.345
  61.9 2.0 %collective-permute-done.10 = f32[2,2,50,1,128]{4,3,0,2,1:T(1,128)S(1)} collective-permute-done((f32[2,2,50,1,128]{4,3,0,2,1:T(1,128)S(1)}, f32[2,2,50,1,128]{4,3,0,2,1:T(1,128)S(1)}, u32[]{:S(2)}, u32[]{:S(2)}) %collective-permute-start.10) | collective-permute-done | bytes 102432 | tf_op jit(solution)/shard_map/ppermute | solution.py:18
  63.9 4.0 %collective-permute-done.11 = f32[2,2,50,1,128]{4,3,0,2,1:T(1,128)S(1)} collective-permute-done((f32[2,2,50,1,128]{4,3,0,2,1:T(1,128)S(1)}, f32[2,2,50,1,128]{4,3,0,2,1:T(1,128)S(1)}, u32[]{:S(2)}, u32[]{:S(2)}) %collective-permute-start.11) | collective-permute-done | bytes 102432 | tf_op jit(solution)/shard_map/ppermute | solution.py:17
  67.9 1.2 fusion.10
  69.1 0.1 fusion.344
  69.2 0.8 collective-permute-start.12
  70.0 0.6 fusion.343
  70.6 1.8 collective-permute-done.12
  72.4 4.4 %collective-permute-done.13 = f32[2,2,50,1,128]{4,3,0,2,1:T(1,128)S(1)} collective-permute-done((f32[2,2,50,1,128]{4,3,0,2,1:T(1,128)S(1)}, f32[2,2,50,1,128]{4,3,0,2,1:T(1,128)S(1)}, u32[]{:S(2)}, u32[]{:S(2)}) %collective-permute-start.13) | collective-permute-done | bytes 102432 | tf_op jit(solution)/shard_map/ppermute | solution.py:17
  76.8 1.2 fusion.3
  78.1 1.0 fusion.43
  79.1 0.1 copy.592
  79.3 0.5 copy-done.7
  79.8 0.1 copy.216
  80.0 100.5 %all-gather.3.cloned.1.call-done = f32[400,16,128]{2,1,0:T(8,128)} async-done(((f32[50,16,128]{2,1,0:T(8,128)}), f32[400,16,128]{2,1,0:T(8,128)}) %all-gather.3.cloned.1.call-update) | async-done | bytes 3276816 | tf_op jit(solution)/shard_map/all_gather | solution.py:121
  180.5 2.2 %reduce_sum.19 = f32[50,16,128]{2,1,0:T(8,128)S(1)} reduce(f32[8,50,16,128]{3,2,1,0:T(8,128)} %bitcast.1268, f32[]{:T(128)} %constant.74.clone.1), dimensions={0}, to_apply=%region_1.0 | reduce | flops 716800 | bytes 3686404 | tf_op jit(solution)/shard_map/reduce_sum | solution.py:121
  182.8 0.8 select_multiply_fusion
  (97 shorter events, 1.0 us)
Async XLA Ops:
  7.2 5.0 %copy-start.3 = (f32[50,16,128]{2,1,0:T(8,128)S(1)}, f32[50,16,128]{2,1,0:T(8,128)}, u32[]{:S(2)}) copy-start(f32[50,16,128]{2,1,0:T(8,128)} %param.24) | copy-start | bytes 1228804
  7.2 173.3 %all-gather.3.cloned.1.call-start = ((), (), s32[]{:S(2)}) async-start(), calls=%async_computation | async-start | bytes 3686400 | tf_op jit(solution)/shard_map/all_gather | solution.py:121
  10.8 1.6 copy-start.9
  12.3 1.4 copy-start
  15.6 5.1 %copy-start.6 = (s32[16,128]{1,0:T(8,128)S(1)}, s32[16,128]{1,0:T(8,128)}, u32[]{:S(2)}) copy-start(s32[16,128]{1,0:T(8,128)} %param.29) | copy-start | bytes 24580
  15.6 5.2 %copy-start.2 = (f32[50,16,128]{2,1,0:T(8,128)S(1)}, f32[50,16,128]{2,1,0:T(8,128)}, u32[]{:S(2)}) copy-start(f32[50,16,128]{2,1,0:T(8,128)} %param.20) | copy-start | bytes 1228804
  16.6 13.1 %collective-permute-start.2 = (f32[2,2,50,1,128]{4,3,0,2,1:T(1,128)S(1)}, f32[2,2,50,1,128]{4,3,0,2,1:T(1,128)S(1)}, u32[]{:S(2)}, u32[]{:S(2)}) collective-permute-start(f32[2,2,50,1,128]{4,3,0,2,1:T(1,128)S(1)} %get-tuple-element.196), channel_id=1, source_target_pairs={{1,0},{2,1},{3,2},{4,3},{5,4},{6,5},{7,6},{8,7},{9,8},{10,9},{11,1... | collective-permute-start | bytes 307208 | tf_op jit(solution)/shard_map/ppermute | solution.py:18
  20.8 9.0 %collective-permute-start.3 = (f32[2,2,50,1,128]{4,3,0,2,1:T(1,128)S(1)}, f32[2,2,50,1,128]{4,3,0,2,1:T(1,128)S(1)}, u32[]{:S(2)}, u32[]{:S(2)}) collective-permute-start(f32[2,2,50,1,128]{4,3,0,2,1:T(1,128)S(1)} %get-tuple-element.197), channel_id=1, source_target_pairs={{0,1},{1,2},{2,3},{3,4},{4,5},{5,6},{6,7},{7,8},{8,9},{9,10},{10,1... | collective-permute-start | bytes 307208 | tf_op jit(solution)/shard_map/ppermute | solution.py:17
  20.9 7.7 %collective-permute-start = (f32[2,50,1,128]{3,2,1,0:T(1,128)S(1)}, f32[2,50,1,128]{3,2,1,0:T(1,128)S(1)}, u32[]{:S(2)}, u32[]{:S(2)}) collective-permute-start(f32[2,50,1,128]{3,2,1,0:T(1,128)S(1)} %get-tuple-element.254), channel_id=1, source_target_pairs={{0,1},{1,2},{2,3},{3,4},{4,5},{5,6},{6,7},{7,8},{8,9},{9,10},{10,1... | collective-permute-start | bytes 153608 | tf_op jit(solution)/shard_map/ppermute | solution.py:17
  21.0 5.2 %copy-start.5 = (f32[50,16,128]{2,1,0:T(8,128)S(1)}, f32[50,16,128]{2,1,0:T(8,128)}, u32[]{:S(2)}) copy-start(f32[50,16,128]{2,1,0:T(8,128)} %param.21) | copy-start | bytes 1228804
  21.0 5.1 %copy-start.11 = (f32[50]{0:T(128)S(1)}, f32[50]{0:T(128)}, u32[]{:S(2)}) copy-start(f32[50]{0:T(128)} %param.23) | copy-start | bytes 604
  21.0 7.6 %collective-permute-start.1 = (f32[2,50,1,128]{3,2,1,0:T(1,128)S(1)}, f32[2,50,1,128]{3,2,1,0:T(1,128)S(1)}, u32[]{:S(2)}, u32[]{:S(2)}) collective-permute-start(f32[2,50,1,128]{3,2,1,0:T(1,128)S(1)} %get-tuple-element.255), channel_id=1, source_target_pairs={{1,0},{2,1},{3,2},{4,3},{5,4},{6,5},{7,6},{8,7},{9,8},{10,9},{11,1... | collective-permute-start | bytes 153608 | tf_op jit(solution)/shard_map/ppermute | solution.py:18
  28.8 0.7 copy-start.12
  31.2 5.5 %collective-permute-start.4 = (f32[2,2,50,1,128]{4,3,0,2,1:T(1,128)S(1)}, f32[2,2,50,1,128]{4,3,0,2,1:T(1,128)S(1)}, u32[]{:S(2)}, u32[]{:S(2)}) collective-permute-start(f32[2,2,50,1,128]{4,3,0,2,1:T(1,128)S(1)} %get-tuple-element.192), channel_id=1, source_target_pairs={{1,0},{2,1},{3,2},{4,3},{5,4},{6,5},{7,6},{8,7},{9,8},{10,9},{11,1... | collective-permute-start | bytes 307208 | tf_op jit(solution)/shard_map/ppermute | solution.py:18
  34.4 7.4 %collective-permute-start.5 = (f32[2,2,50,1,128]{4,3,0,2,1:T(1,128)S(1)}, f32[2,2,50,1,128]{4,3,0,2,1:T(1,128)S(1)}, u32[]{:S(2)}, u32[]{:S(2)}) collective-permute-start(f32[2,2,50,1,128]{4,3,0,2,1:T(1,128)S(1)} %get-tuple-element.193), channel_id=1, source_target_pairs={{0,1},{1,2},{2,3},{3,4},{4,5},{5,6},{6,7},{7,8},{8,9},{9,10},{10,1... | collective-permute-start | bytes 307208 | tf_op jit(solution)/shard_map/ppermute | solution.py:17
  43.2 3.2 %collective-permute-start.6 = (f32[2,2,50,1,128]{4,3,0,2,1:T(1,128)S(1)}, f32[2,2,50,1,128]{4,3,0,2,1:T(1,128)S(1)}, u32[]{:S(2)}, u32[]{:S(2)}) collective-permute-start(f32[2,2,50,1,128]{4,3,0,2,1:T(1,128)S(1)} %get-tuple-element.188), channel_id=1, source_target_pairs={{1,0},{2,1},{3,2},{4,3},{5,4},{6,5},{7,6},{8,7},{9,8},{10,9},{11,1... | collective-permute-start | bytes 307208 | tf_op jit(solution)/shard_map/ppermute | solution.py:18
  43.3 7.0 %collective-permute-start.7 = (f32[2,2,50,1,128]{4,3,0,2,1:T(1,128)S(1)}, f32[2,2,50,1,128]{4,3,0,2,1:T(1,128)S(1)}, u32[]{:S(2)}, u32[]{:S(2)}) collective-permute-start(f32[2,2,50,1,128]{4,3,0,2,1:T(1,128)S(1)} %get-tuple-element.189), channel_id=1, source_target_pairs={{0,1},{1,2},{2,3},{3,4},{4,5},{5,6},{6,7},{7,8},{8,9},{9,10},{10,1... | collective-permute-start | bytes 307208 | tf_op jit(solution)/shard_map/ppermute | solution.py:17
  51.6 3.2 %collective-permute-start.8 = (f32[2,2,50,1,128]{4,3,0,2,1:T(1,128)S(1)}, f32[2,2,50,1,128]{4,3,0,2,1:T(1,128)S(1)}, u32[]{:S(2)}, u32[]{:S(2)}) collective-permute-start(f32[2,2,50,1,128]{4,3,0,2,1:T(1,128)S(1)} %get-tuple-element.184), channel_id=1, source_target_pairs={{1,0},{2,1},{3,2},{4,3},{5,4},{6,5},{7,6},{8,7},{9,8},{10,9},{11,1... | collective-permute-start | bytes 307208 | tf_op jit(solution)/shard_map/ppermute | solution.py:18
  52.5 6.8 %collective-permute-start.9 = (f32[2,2,50,1,128]{4,3,0,2,1:T(1,128)S(1)}, f32[2,2,50,1,128]{4,3,0,2,1:T(1,128)S(1)}, u32[]{:S(2)}, u32[]{:S(2)}) collective-permute-start(f32[2,2,50,1,128]{4,3,0,2,1:T(1,128)S(1)} %get-tuple-element.185), channel_id=1, source_target_pairs={{0,1},{1,2},{2,3},{3,4},{4,5},{5,6},{6,7},{7,8},{8,9},{9,10},{10,1... | collective-permute-start | bytes 307208 | tf_op jit(solution)/shard_map/ppermute | solution.py:17
  60.7 3.2 %collective-permute-start.10 = (f32[2,2,50,1,128]{4,3,0,2,1:T(1,128)S(1)}, f32[2,2,50,1,128]{4,3,0,2,1:T(1,128)S(1)}, u32[]{:S(2)}, u32[]{:S(2)}) collective-permute-start(f32[2,2,50,1,128]{4,3,0,2,1:T(1,128)S(1)} %get-tuple-element.180), channel_id=1, source_target_pairs={{1,0},{2,1},{3,2},{4,3},{5,4},{6,5},{7,6},{8,7},{9,8},{10,9},{11,1... | collective-permute-start | bytes 307208 | tf_op jit(solution)/shard_map/ppermute | solution.py:18
  60.9 7.0 %collective-permute-start.11 = (f32[2,2,50,1,128]{4,3,0,2,1:T(1,128)S(1)}, f32[2,2,50,1,128]{4,3,0,2,1:T(1,128)S(1)}, u32[]{:S(2)}, u32[]{:S(2)}) collective-permute-start(f32[2,2,50,1,128]{4,3,0,2,1:T(1,128)S(1)} %get-tuple-element.181), channel_id=1, source_target_pairs={{0,1},{1,2},{2,3},{3,4},{4,5},{5,6},{6,7},{7,8},{8,9},{9,10},{10,1... | collective-permute-start | bytes 307208 | tf_op jit(solution)/shard_map/ppermute | solution.py:17
  69.2 3.2 %collective-permute-start.12 = (f32[2,2,50,1,128]{4,3,0,2,1:T(1,128)S(1)}, f32[2,2,50,1,128]{4,3,0,2,1:T(1,128)S(1)}, u32[]{:S(2)}, u32[]{:S(2)}) collective-permute-start(f32[2,2,50,1,128]{4,3,0,2,1:T(1,128)S(1)} %get-tuple-element.176), channel_id=1, source_target_pairs={{1,0},{2,1},{3,2},{4,3},{5,4},{6,5},{7,6},{8,7},{9,8},{10,9},{11,1... | collective-permute-start | bytes 307208 | tf_op jit(solution)/shard_map/ppermute | solution.py:18
  70.0 6.8 %collective-permute-start.13 = (f32[2,2,50,1,128]{4,3,0,2,1:T(1,128)S(1)}, f32[2,2,50,1,128]{4,3,0,2,1:T(1,128)S(1)}, u32[]{:S(2)}, u32[]{:S(2)}) collective-permute-start(f32[2,2,50,1,128]{4,3,0,2,1:T(1,128)S(1)} %get-tuple-element.177), channel_id=1, source_target_pairs={{0,1},{1,2},{2,3},{3,4},{4,5},{5,6},{6,7},{7,8},{8,9},{9,10},{10,1... | collective-permute-start | bytes 307208 | tf_op jit(solution)/shard_map/ppermute | solution.py:17
  78.1 1.0 copy-start.10
  79.1 0.7 copy-start.7
  79.1 0.7 copy-start.8
  80.0 102.7 %copy-start.1 = (f32[2,2,50,16,128]{4,3,2,1,0:T(8,128)}, f32[2,2,50,16,128]{4,3,2,1,0:T(8,128)S(1)}, u32[]{:S(2)}) copy-start(f32[2,2,50,16,128]{4,3,2,1,0:T(8,128)S(1)} %fusion.142) | copy-start | bytes 4915204
  180.5 2.2 %copy-start.4 = (f32[50,16,128]{2,1,0:T(8,128)S(1)}, f32[50,16,128]{2,1,0:T(8,128)}, u32[]{:S(2)}) copy-start(f32[50,16,128]{2,1,0:T(8,128)} %param.26) | copy-start | bytes 1228804
Sparse Core Ops, SparseCore 0:
  79.2 101.2 all-gather.2
